TPU v7x, 512 devices: a whole 4x4x16 slice. The times are simulated.
512 devices in a mesh: exp: 16 (over z), sky: 32 (over y, x, core).
Axes of the slice: x: 4, y: 4, z: 16, core: 2. Of those that a mesh axis runs over, the one named last changes fastest.
Arguments:
- sky_start: float32 [16, 128, 4096], P(None, None, 'sky'), may hold values from -6 to 6
- exposures: bfloat16 [16, 1024, 2, 128, 128], P('exp', 'sky'), may hold values from -16 to 16
- weights: bfloat16 [16, 1024, 2], P('exp', 'sky'), may hold values from 0.5 to 2
- footprint_owner: int32 [16, 1024, 1], P('exp', 'sky'), may hold values from 0 to 31; in each aligned block of 32 rows (0 to 31, 32 to 63, ..., all dimensions but the last counted through in order) at most 2 rows name the same one
- footprint_row: int32 [16, 1024], P('exp', 'sky'), may hold values from 0 to 15
- kernel_index: int32 [16, 1024, 2, 2], P('exp', 'sky'), may hold values from 0 to 7
- kernels: bfloat16 [8, 128, 128], replicated, may hold values from -1 to 1
Outputs:
- sky_image: float32 [16, 128, 4096], P(None, None, 'sky')
Inputs may be any that keep to these rules, and one draw needn't show every extreme that they name: `footprint_owner`: the 32 footprint tiles of one device name one tile column at most 2 times, and some tile column exactly 2 times.
All inputs are finite; a program needn't handle non-finite values.
Results may differ from a plain program's by a relative error of at most 0.0035.
Values may be sent and summed in bfloat16 or wider, within the bound.
No kernel may reach another device: no remote copies, remote signals or barrier semaphores. Data moves between devices by JAX's collectives and lax.ppermute only.
A program may use at most 128 MiB of HBM per device.

v0:
```python
import jax
import jax.numpy as jnp
from jax import lax
from jax.sharding import PartitionSpec as P

ITERS = 2
weight_ceiling = 2.0


def padded_2(cells, sides, width):
    for axis, dim in sides:
        count = lax.axis_size(axis)
        ends = count - 1
        head = lax.slice_in_dim(cells, 0, width, axis=dim)
        tail = lax.slice_in_dim(cells, cells.shape[dim] - width, cells.shape[dim], axis=dim)
        cells = jnp.concatenate(
            [
                lax.ppermute(tail, axis, [(i, (i + 1) % count) for i in range(ends)]),
                cells,
                lax.ppermute(head, axis, [((i + 1) % count, i) for i in range(ends)]),
            ],
            axis=dim,
        )
    return cells


def pick_kernels(kernel_ids, kernels):
    table_size = kernels.shape[0]
    tile_edge = kernels.shape[1]
    onehot = (kernel_ids[..., None] == jnp.arange(table_size, dtype=jnp.int32)).astype(jnp.bfloat16)
    onehot = onehot.reshape(-1, table_size)
    selected = jnp.dot(onehot, kernels.reshape(table_size, -1), preferred_element_type=jnp.float32)
    selected = selected.astype(jnp.bfloat16).reshape(kernel_ids.shape + (tile_edge, tile_edge))
    return (selected[..., 0, :, :], selected[..., 1, :, :])


def adjoint_tiles(fetched, left_kernels, right_kernels, tile_weights, observed):
    left_product = jnp.einsum(
        "fetu,fuv->fetv", left_kernels, fetched, preferred_element_type=jnp.float32
    ).astype(jnp.bfloat16)
    predicted = jnp.einsum(
        "fetv,fewv->fetw", left_product, right_kernels, preferred_element_type=jnp.float32
    )
    residual = tile_weights.astype(jnp.float32)[..., None, None] * (
        predicted - observed.astype(jnp.float32)
    )
    residual = residual.astype(jnp.bfloat16)
    back_product = jnp.einsum(
        "feut,feuw->fetw", left_kernels, residual, preferred_element_type=jnp.float32
    ).astype(jnp.bfloat16)
    summed = jnp.sum(
        jnp.einsum(
            "fetw,fewv->fetv", back_product, right_kernels, preferred_element_type=jnp.float32
        ),
        axis=1,
    )
    return summed.astype(jnp.bfloat16)


def laplace_image(padded):
    image_rows = padded.reshape(padded.shape[0] * padded.shape[1], padded.shape[2])
    center = image_rows[:, 1:-1]
    vertical = jnp.pad(center, ((1, 1), (0, 0)))
    laplacian = 4.0 * center - image_rows[:, :-2] - image_rows[:, 2:] - vertical[:-2] - vertical[2:]
    return laplacian.reshape(padded.shape[0], padded.shape[1], padded.shape[2] - 2)


def per_device(
    sky_start, exposures, weights, footprint_owner, footprint_row, kernel_index, kernels
):
    sky_rows = sky_start.shape[0]
    tile_edge = sky_start.shape[1]
    foot_tiles = footprint_row.shape[1]
    expo_count = exposures.shape[2]
    n_sky = lax.axis_size("sky")
    n_exp = lax.axis_size("exp")
    capacity = max(2, 3 * foot_tiles // (2 * n_sky))
    slot_count = n_sky * capacity
    prior_weight = n_exp * foot_tiles * expo_count / (8.0 * sky_rows)
    owner_ids = footprint_owner[0, :, 0]
    tile_rows = footprint_row[0]
    onehot_owner = (owner_ids[:, None] == jnp.arange(n_sky, dtype=jnp.int32)[None, :]).astype(
        jnp.int32
    )
    ranks = jnp.sum((jnp.cumsum(onehot_owner, axis=0) - onehot_owner) * onehot_owner, axis=1)
    slot_of = owner_ids * capacity + ranks
    packing = jnp.arange(slot_count, dtype=jnp.int32)[:, None] == slot_of[None, :]
    requested = jnp.sum(jnp.where(packing, tile_rows[None, :] + 1, 0), axis=1) - 1
    slot_source = jnp.sum(jnp.where(packing, jnp.arange(foot_tiles)[None, :] + 1, 0), axis=1) - 1
    slot_source = jnp.where(slot_source < 0, foot_tiles, slot_source)
    observed = exposures[0]
    tile_weights = weights[0]
    kernel_ids = kernel_index[0]
    incoming = lax.all_to_all(requested, "sky", split_axis=0, concat_axis=0, tiled=True)
    left_kernels, right_kernels = pick_kernels(kernel_ids, kernels)
    receive_map = jnp.arange(sky_rows, dtype=jnp.int32)[:, None] == incoming[None, :]
    local_counts = float(expo_count) * jnp.sum(receive_map.astype(jnp.float32), axis=1)
    receive_half = receive_map.astype(jnp.bfloat16)
    safe_rows = jnp.maximum(incoming, 0)
    rows_per = sky_rows // n_exp
    own_rows = lax.axis_index("exp") * rows_per
    count_block = jnp.broadcast_to(
        local_counts.astype(jnp.bfloat16)[None, :, None], (n_exp, sky_rows, tile_edge)
    )
    half_edge = tile_edge // 2

    def exchange(outgoing_rows, extra, arrived_already=False):
        arrived = outgoing_rows
        if not arrived_already:
            arrived = lax.all_to_all(outgoing_rows, "sky", split_axis=0, concat_axis=0, tiled=True)
        partial_value = jnp.einsum(
            "rj,juv->ruv", receive_half, arrived, preferred_element_type=jnp.float32
        )
        payload = partial_value.astype(jnp.bfloat16).reshape(
            n_exp, rows_per * outgoing_rows.shape[1], tile_edge
        )
        if extra is not None:
            payload = jnp.concatenate([payload, extra], axis=1)
        row_parts = lax.all_to_all(payload, "exp", split_axis=0, concat_axis=0, tiled=True)
        return jnp.sum(row_parts.astype(jnp.float32).reshape((n_exp,) + payload.shape[1:]), axis=0)

    def fetch(part):
        replies = lax.all_to_all(
            part.astype(jnp.bfloat16)[safe_rows], "sky", split_axis=0, concat_axis=0, tiled=True
        )
        return replies[slot_of]

    def gather_scaled(summed, own_denominator):
        piece_edge = summed.shape[0] // rows_per
        own_total = summed.reshape(rows_per, piece_edge, tile_edge)
        scaled = (own_total / own_denominator[:, None, None]).astype(jnp.bfloat16)
        return scaled

    sky_now = sky_start
    fetched = None
    for iteration in range(ITERS):
        if fetched is None:
            fetched = fetch(sky_now)
        adjoint = adjoint_tiles(fetched, left_kernels, right_kernels, tile_weights, observed)
        padded_adjoint = jnp.concatenate(
            [adjoint, jnp.zeros((1, tile_edge, tile_edge), adjoint.dtype)], axis=0
        )
        outgoing = padded_adjoint[slot_source]
        laplacian = laplace_image(padded_2(sky_now, (("sky", 2),), 1))
        if iteration == 0:
            summed = exchange(outgoing[:, :half_edge], count_block)
            counts = summed[rows_per * half_edge :, 0]
            denominator = weight_ceiling * counts + 8.0 * prior_weight
            own_denominator = lax.dynamic_slice_in_dim(denominator, own_rows, rows_per)
            summed_head = summed[: rows_per * half_edge]
            smooth = prior_weight * laplacian / denominator[:, None, None]
        else:
            smooth = prior_weight * laplacian / denominator[:, None, None]
            if iteration + 1 == ITERS:
                scaled = gather_scaled(exchange(outgoing, None), own_denominator)
                gathered = lax.all_gather(scaled, "exp", axis=0, tiled=True)
                sky_now = sky_now - (gathered.astype(jnp.float32) + smooth)
                continue
            summed_head = exchange(outgoing[:, :half_edge], None)
        scaled_head = gather_scaled(summed_head, own_denominator)
        scaled_head, outgoing_tail = lax.optimization_barrier(
            (scaled_head, outgoing[:, half_edge:])
        )
        gathered_head = lax.all_gather(scaled_head, "exp", axis=0, tiled=True)
        arrived_tail = lax.all_to_all(outgoing_tail, "sky", split_axis=0, concat_axis=0, tiled=True)
        gathered_head, arrived_tail = lax.optimization_barrier((gathered_head, arrived_tail))
        scaled_tail = gather_scaled(exchange(arrived_tail, None, True), own_denominator)
        sky_head = sky_now[:, :half_edge] - (
            gathered_head.astype(jnp.float32) + smooth[:, :half_edge]
        )
        if iteration + 1 == ITERS:
            gathered_tail = lax.all_gather(scaled_tail, "exp", axis=0, tiled=True)
            sky_tail = sky_now[:, half_edge:] - (
                gathered_tail.astype(jnp.float32) + smooth[:, half_edge:]
            )
            sky_now = jnp.concatenate([sky_head, sky_tail], axis=1)
            continue
        request_head = sky_head.astype(jnp.bfloat16)[safe_rows]
        request_head, scaled_tail = lax.optimization_barrier((request_head, scaled_tail))
        gathered_tail = lax.all_gather(scaled_tail, "exp", axis=0, tiled=True)
        fetched_head = lax.all_to_all(request_head, "sky", split_axis=0, concat_axis=0, tiled=True)[
            slot_of
        ]
        gathered_tail, fetched_head = lax.optimization_barrier((gathered_tail, fetched_head))
        sky_tail = sky_now[:, half_edge:] - (
            gathered_tail.astype(jnp.float32) + smooth[:, half_edge:]
        )
        fetched = jnp.concatenate([fetched_head, fetch(sky_tail)], axis=1)
        sky_now = jnp.concatenate([sky_head, sky_tail], axis=1)
    return sky_now


def solution(mesh):
    in_specs = (
        P(None, None, "sky"),
        P("exp", "sky", None, None, None),
        P("exp", "sky", None),
        P("exp", "sky", None),
        P("exp", "sky"),
        P("exp", "sky", None, None),
        P(),
    )
    out_specs = P(None, None, "sky")
    return jax.shard_map(
        per_device, mesh=mesh, in_specs=in_specs, out_specs=out_specs, check_vma=False
    )
```

profile of v0, /device:TPU:2, one launch (start us, length us, event | category | flops | bytes accessed | tf_op | source)
XLA Modules:
  0.0 392.2 jit_solution(12822003709473119195)
XLA Ops:
  3.8 9.4 %all-to-all-start = ((s32[32,2,1]{1,2,0:T(1,128)}), s32[32,2,1]{1,2,0:T(1,128)S(1)}, u32[]{:S(2)}, u32[]{:S(2)}) async-start(s32[32,2,1]{1,2,0:T(1,128)} %bitcast.2), calls=%async_computation | async-start | bytes 32768 | tf_op jit(solution)/shard_map/all_to_all | solution.py:94
  13.2 1.3 convert_element_type.137
  14.5 4.9 %all-to-all-done = s32[32,2,1]{1,2,0:T(1,128)S(1)} async-done(((s32[32,2,1]{1,2,0:T(1,128)}), s32[32,2,1]{1,2,0:T(1,128)S(1)}, u32[]{:S(2)}, u32[]{:S(2)}) %all-to-all-start) | async-done | bytes 288 | tf_op jit(solution)/shard_map/all_to_all | solution.py:94
  20.7 2.1 gather_fusion
  22.9 5.2 %all-to-all-start.1 = ((bf16[64,128,128]{2,1,0:T(8,128)(2,1)}), bf16[64,128,128]{2,1,0:T(8,128)(2,1)S(1)}, u32[]{:S(2)}, u32[]{:S(2)}) async-start(bf16[64,128,128]{2,1,0:T(8,128)(2,1)} %gather_fusion), calls=%async_computation.1 | async-start | bytes 4194304 | tf_op jit(solution)/shard_map/all_to_all | solution.py:123
  28.5 1.3 fusion.4
  29.8 3.2 copy.72
  33.0 23.1 %all-to-all-done.1 = bf16[64,128,128]{2,1,0:T(8,128)(2,1)S(1)} async-done(((bf16[64,128,128]{2,1,0:T(8,128)(2,1)}), bf16[64,128,128]{2,1,0:T(8,128)(2,1)S(1)}, u32[]{:S(2)}, u32[]{:S(2)}) %all-to-all-start.1) | async-done | bytes 2097184 | tf_op jit(solution)/shard_map/all_to_all | solution.py:123
  56.8 6.3 %fusion.1 = bf16[32,2,128,128]{3,2,1,0:T(8,128)(2,1)} fusion(bf16[1,32,2,128,128]{4,3,2,1,0:T(8,128)(2,1)} %param.8, f32[32,2]{1,0:T(8,128)S(1)} %copy.43, bf16[32,2,2,128,128]{4,3,2,1,0:T(8,128)(2,1)} %bitcast.93, bf16[32,128,128]{2,1,0:T(8,128)(2,1)S(1)} %gather_fusion.1), kind=kOutput, calls=%fused_computation.12 | convolution fusion | flops 542113792 | bytes 9437440 | tf_op jit(solution)/shard_map/fetv,fewv->fetw/dot_general | solution.py:41
  63.2 4.3 %bitcast_convert_fusion.1 = bf16[32,128,128]{2,1,0:T(8,128)(2,1)S(1)} fusion(bf16[32,2,128,128]{3,2,1,0:T(8,128)(2,1)} %fusion.1, bf16[32,2,2,128,128]{4,3,2,1,0:T(8,128)(2,1)} %bitcast.94), kind=kOutput, calls=%fused_computation.21 | convolution fusion | flops 538443776 | bytes 7340032 | tf_op jit(solution)/shard_map/fetw,fewv->fetv/dot_general | solution.py:52
  67.6 1.0 gather_fusion.2
  68.5 1.5 fusion.72
  70.0 5.9 %all-to-all-start.2 = ((bf16[64,64,128]{2,1,0:T(8,128)(2,1)}), bf16[64,64,128]{2,1,0:T(8,128)(2,1)S(1)}, u32[]{:S(2)}, u32[]{:S(2)}) async-start(bf16[64,64,128]{2,1,0:T(8,128)(2,1)} %get-tuple-element.30), calls=%async_computation.2 | async-start | bytes 2097152 | tf_op jit(solution)/shard_map/all_to_all | solution.py:110
  76.3 15.9 %all-to-all-done.2 = bf16[64,64,128]{2,1,0:T(8,128)(2,1)S(1)} async-done(((bf16[64,64,128]{2,1,0:T(8,128)(2,1)}), bf16[64,64,128]{2,1,0:T(8,128)(2,1)S(1)}, u32[]{:S(2)}, u32[]{:S(2)}) %all-to-all-start.2) | async-done | bytes 1048608 | tf_op jit(solution)/shard_map/all_to_all | solution.py:110
  93.9 13.3 %all-to-all-start.3 = ((bf16[16,80,128]{2,1,0:T(8,128)(2,1)}), bf16[16,80,128]{2,1,0:T(8,128)(2,1)S(1)}, u32[]{:S(2)}, u32[]{:S(2)}) async-start(bf16[16,80,128]{2,1,0:T(8,128)(2,1)} %copy.47), calls=%async_computation.3 | async-start | bytes 655360 | tf_op jit(solution)/shard_map/all_to_all | solution.py:119
  107.2 21.4 %all-to-all-done.3 = bf16[16,80,128]{2,1,0:T(8,128)(2,1)S(1)} async-done(((bf16[16,80,128]{2,1,0:T(8,128)(2,1)}), bf16[16,80,128]{2,1,0:T(8,128)(2,1)S(1)}, u32[]{:S(2)}, u32[]{:S(2)}) %all-to-all-start.3) | async-done | bytes 327712 | tf_op jit(solution)/shard_map/all_to_all | solution.py:119
  129.9 5.6 %all-to-all-start.4 = ((bf16[64,64,128]{2,1,0:T(8,128)(2,1)}), bf16[64,64,128]{2,1,0:T(8,128)(2,1)}, u32[]{:S(2)}, u32[]{:S(2)}) async-start(bf16[64,64,128]{2,1,0:T(8,128)(2,1)} %get-tuple-element.14), calls=%async_computation.4 | async-start | bytes 2097152 | tf_op jit(solution)/shard_map/all_to_all | solution.py:165
  136.3 2.0 collective-permute-start.1
  138.6 2.5 collective-permute-start
  141.1 6.4 %collective-permute-done.1 = f32[16,128,1]{1,0,2:T(8,128)S(1)} collective-permute-done((f32[16,128,1]{1,0,2:T(8,128)S(1)}, f32[16,128,1]{1,0,2:T(8,128)S(1)}, u32[]{:S(2)}, u32[]{:S(2)}) %collective-permute-start.1) | collective-permute-done | bytes 8224 | tf_op jit(solution)/shard_map/ppermute | solution.py:20
  147.5 1.3 copy.51
  148.8 1.4 copy.50
  150.2 2.4 pad_maximum_fusion
  152.6 1.3 slice.118
  153.9 33.8 %all_gather.9 = bf16[16,64,128]{2,1,0:T(8,128)(2,1)} all-gather(bf16[1,64,128]{2,1,0:T(8,128)(2,1)S(1)} %fusion.53), channel_id=1, replica_groups=mesh['exp'=16,'sky'=32] {'exp'}, dimensions={0}, use_global_device_ids=true | all-gather | bytes 278528 | tf_op jit(solution)/shard_map/all_gather | solution.py:164
  187.8 1.9 convolution_convert_fusion.1
  190.5 4.5 %all-to-all-start.5 = ((bf16[16,64,128]{2,1,0:T(8,128)(2,1)}), bf16[16,64,128]{2,1,0:T(8,128)(2,1)S(1)}, u32[]{:S(2)}, u32[]{:S(2)}) async-start(bf16[16,64,128]{2,1,0:T(8,128)(2,1)} %copy.53), calls=%async_computation.5 | async-start | bytes 524288 | tf_op jit(solution)/shard_map/all_to_all | solution.py:119
  194.9 2.5 fusion.36
  199.3 1.6 gather_fusion.3
  201.0 8.2 %all-to-all-done.5 = bf16[16,64,128]{2,1,0:T(8,128)(2,1)S(1)} async-done(((bf16[16,64,128]{2,1,0:T(8,128)(2,1)}), bf16[16,64,128]{2,1,0:T(8,128)(2,1)S(1)}, u32[]{:S(2)}, u32[]{:S(2)}) %all-to-all-start.5) | async-done | bytes 262176 | tf_op jit(solution)/shard_map/all_to_all | solution.py:119
  209.8 7.9 %all-to-all-start.6 = ((bf16[64,64,128]{2,1,0:T(8,128)(2,1)}), bf16[64,64,128]{2,1,0:T(8,128)(2,1)S(1)}, u32[]{:S(2)}, u32[]{:S(2)}) async-start(bf16[64,64,128]{2,1,0:T(8,128)(2,1)} %gather_fusion.3), calls=%async_computation.6 | async-start | bytes 2097152 | tf_op jit(solution)/shard_map/all_to_all | solution.py:181
  217.7 31.1 %all_gather.10 = bf16[16,64,128]{2,1,0:T(8,128)(2,1)S(1)} all-gather(bf16[1,64,128]{2,1,0:T(8,128)(2,1)S(1)} %fusion.52), channel_id=1, replica_groups=mesh['exp'=16,'sky'=32] {'exp'}, dimensions={0}, use_global_device_ids=true | all-gather | bytes 278528 | tf_op jit(solution)/shard_map/all_gather | solution.py:180
  248.8 1.4 gather_fusion.4
  251.9 23.4 %all_to_all.51 = bf16[64,64,128]{2,1,0:T(8,128)(2,1)S(1)} all-to-all(bf16[64,64,128]{2,1,0:T(8,128)(2,1)S(1)} %gather_fusion.5), channel_id=1, replica_groups=mesh['exp'=16,'sky'=32] {'sky'}, dimensions={0} | all-to-all | bytes 2097152 | tf_op jit(solution)/shard_map/all_to_all | solution.py:123
  276.0 6.3 %fusion.3 = bf16[32,2,128,128]{3,2,1,0:T(8,128)(2,1)} fusion(bf16[1,32,2,128,128]{4,3,2,1,0:T(8,128)(2,1)} %param.8, f32[32,2]{1,0:T(8,128)S(1)} %copy.43, bf16[32,2,2,128,128]{4,3,2,1,0:T(8,128)(2,1)} %bitcast.95, bf16[32,64,128]{2,1,0:T(8,128)(2,1)S(1)} %gather_fusion.6, bf16[32,64,128]{2,1,0:T(8,128)(2,1)S(1)} %copy-done.4), kind=kOutput, calls=%fused_computation.14 | convolution fusion | flops 544210944 | bytes 9437440 | tf_op jit(solution)/shard_map/fetv,fewv->fetw/dot_general | solution.py:41
  282.3 4.3 %bitcast_convert_fusion = bf16[32,128,128]{2,1,0:T(8,128)(2,1)S(1)} fusion(bf16[32,2,128,128]{3,2,1,0:T(8,128)(2,1)} %fusion.3, bf16[32,2,2,128,128]{4,3,2,1,0:T(8,128)(2,1)} %bitcast.96), kind=kOutput, calls=%fused_computation.20 | convolution fusion | flops 538443776 | bytes 7340032 | tf_op jit(solution)/shard_map/fetw,fewv->fetv/dot_general | solution.py:52
  286.7 1.0 gather_fusion.7
  287.7 31.9 %all_to_all.52 = bf16[64,128,128]{2,1,0:T(8,128)(2,1)S(1)} all-to-all(bf16[64,128,128]{2,1,0:T(8,128)(2,1)S(1)} %gather_fusion.7), channel_id=1, replica_groups=mesh['exp'=16,'sky'=32] {'sky'}, dimensions={0} | all-to-all | bytes 4194304 | tf_op jit(solution)/shard_map/all_to_all | solution.py:110
  319.6 1.3 fusion.25
  320.8 0.9 copy.56
  321.8 4.3 %all-to-all-start.9 = ((bf16[16,128,128]{2,1,0:T(8,128)(2,1)}), bf16[16,128,128]{2,1,0:T(8,128)(2,1)}, u32[]{:S(2)}, u32[]{:S(2)}) async-start(bf16[16,128,128]{2,1,0:T(8,128)(2,1)} %copy.56), calls=%async_computation.9 | async-start | bytes 1048576 | tf_op jit(solution)/shard_map/all_to_all | solution.py:119
  326.8 3.1 collective-permute-start.3
  330.2 2.1 collective-permute-start.2
  332.7 2.4 collective-permute-done.2
  337.2 18.3 %all-to-all-done.9 = bf16[16,128,128]{2,1,0:T(8,128)(2,1)} async-done(((bf16[16,128,128]{2,1,0:T(8,128)(2,1)}), bf16[16,128,128]{2,1,0:T(8,128)(2,1)}, u32[]{:S(2)}, u32[]{:S(2)}) %all-to-all-start.9) | async-done | bytes 524320 | tf_op jit(solution)/shard_map/all_to_all | solution.py:119
  355.5 1.1 convert_reduce_fusion
  357.2 33.7 %all-gather = bf16[2048,128]{1,0:T(8,128)(2,1)S(1)} all-gather(bf16[128,128]{1,0:T(8,128)(2,1)S(1)} %divide_convert_fusion), channel_id=2, replica_groups=mesh['exp'=16,'sky'=32] {'exp'}, dimensions={0}, use_global_device_ids=true | all-gather | bytes 557056 | tf_op jit(solution)/shard_map/all_gather | solution.py:156
  391.0 1.2 fusion.30
  (76 shorter events, 20.4 us)
Async XLA Ops:
  3.8 15.6 %all-to-all-start = ((s32[32,2,1]{1,2,0:T(1,128)}), s32[32,2,1]{1,2,0:T(1,128)S(1)}, u32[]{:S(2)}, u32[]{:S(2)}) async-start(s32[32,2,1]{1,2,0:T(1,128)} %bitcast.2), calls=%async_computation | async-start | bytes 32768 | tf_op jit(solution)/shard_map/all_to_all | solution.py:94
  22.8 5.3 %copy-start.8 = (bf16[1,32,2]{1,2,0:T(2,128)(2,1)S(1)}, bf16[1,32,2]{1,2,0:T(2,128)(2,1)}, u32[]{:S(2)}) copy-start(bf16[1,32,2]{1,2,0:T(2,128)(2,1)} %param.9) | copy-start | bytes 388
  22.8 5.4 %copy-start.7 = (s32[1,32,2,2]{1,3,2,0:T(2,128)S(1)}, s32[1,32,2,2]{1,3,2,0:T(2,128)}, u32[]{:S(2)}) copy-start(s32[1,32,2,2]{1,3,2,0:T(2,128)} %param.12) | copy-start | bytes 1540
  22.8 5.6 %copy-start.5 = (bf16[8,128,128]{2,1,0:T(8,128)(2,1)S(1)}, bf16[8,128,128]{2,1,0:T(8,128)(2,1)}, u32[]{:S(2)}) copy-start(bf16[8,128,128]{2,1,0:T(8,128)(2,1)} %param.13) | copy-start | bytes 786436
  22.9 33.2 %all-to-all-start.1 = ((bf16[64,128,128]{2,1,0:T(8,128)(2,1)}), bf16[64,128,128]{2,1,0:T(8,128)(2,1)S(1)}, u32[]{:S(2)}, u32[]{:S(2)}) async-start(bf16[64,128,128]{2,1,0:T(8,128)(2,1)} %gather_fusion), calls=%async_computation.1 | async-start | bytes 4194304 | tf_op jit(solution)/shard_map/all_to_all | solution.py:123
  29.8 3.2 copy-start.6
  70.0 22.2 %all-to-all-start.2 = ((bf16[64,64,128]{2,1,0:T(8,128)(2,1)}), bf16[64,64,128]{2,1,0:T(8,128)(2,1)S(1)}, u32[]{:S(2)}, u32[]{:S(2)}) async-start(bf16[64,64,128]{2,1,0:T(8,128)(2,1)} %get-tuple-element.30), calls=%async_computation.2 | async-start | bytes 2097152 | tf_op jit(solution)/shard_map/all_to_all | solution.py:110
  92.9 42.7 %copy-start = (f32[16,128,128]{2,1,0:T(8,128)S(1)}, f32[16,128,128]{2,1,0:T(8,128)}, u32[]{:S(2)}) copy-start(f32[16,128,128]{2,1,0:T(8,128)} %param.7) | copy-start | bytes 3145732
  93.9 34.7 %all-to-all-start.3 = ((bf16[16,80,128]{2,1,0:T(8,128)(2,1)}), bf16[16,80,128]{2,1,0:T(8,128)(2,1)S(1)}, u32[]{:S(2)}, u32[]{:S(2)}) async-start(bf16[16,80,128]{2,1,0:T(8,128)(2,1)} %copy.47), calls=%async_computation.3 | async-start | bytes 655360 | tf_op jit(solution)/shard_map/all_to_all | solution.py:119
  129.9 57.8 %all-to-all-start.4 = ((bf16[64,64,128]{2,1,0:T(8,128)(2,1)}), bf16[64,64,128]{2,1,0:T(8,128)(2,1)}, u32[]{:S(2)}, u32[]{:S(2)}) async-start(bf16[64,64,128]{2,1,0:T(8,128)(2,1)} %get-tuple-element.14), calls=%async_computation.4 | async-start | bytes 2097152 | tf_op jit(solution)/shard_map/all_to_all | solution.py:165
  136.3 11.2 %collective-permute-start.1 = (f32[16,128,1]{1,0,2:T(8,128)S(1)}, f32[16,128,1]{1,0,2:T(8,128)S(1)}, u32[]{:S(2)}, u32[]{:S(2)}) collective-permute-start(f32[16,128,1]{1,0,2:T(8,128)S(1)} %copy.70), channel_id=1, source_target_pairs={{1,0},{2,1},{3,2},{4,3},{5,4},{6,5},{7,6},{8,7},{9,8},{10,9},{11,1... | collective-permute-start | bytes 24584 | tf_op jit(solution)/shard_map/ppermute | solution.py:20
  138.6 10.2 %collective-permute-start = (f32[16,128,1]{1,0,2:T(8,128)S(1)}, f32[16,128,1]{1,0,2:T(8,128)S(1)}, u32[]{:S(2)}, u32[]{:S(2)}) collective-permute-start(f32[16,128,1]{1,0,2:T(8,128)S(1)} %copy.69), channel_id=1, source_target_pairs={{0,1},{1,2},{2,3},{3,4},{4,5},{5,6},{6,7},{7,8},{8,9},{9,10},{10,1... | collective-permute-start | bytes 24584 | tf_op jit(solution)/shard_map/ppermute | solution.py:18
  190.5 18.7 %all-to-all-start.5 = ((bf16[16,64,128]{2,1,0:T(8,128)(2,1)}), bf16[16,64,128]{2,1,0:T(8,128)(2,1)S(1)}, u32[]{:S(2)}, u32[]{:S(2)}) async-start(bf16[16,64,128]{2,1,0:T(8,128)(2,1)} %copy.53), calls=%async_computation.5 | async-start | bytes 524288 | tf_op jit(solution)/shard_map/all_to_all | solution.py:119
  197.5 1.0 copy-start.3
  209.8 39.0 %all-to-all-start.6 = ((bf16[64,64,128]{2,1,0:T(8,128)(2,1)}), bf16[64,64,128]{2,1,0:T(8,128)(2,1)S(1)}, u32[]{:S(2)}, u32[]{:S(2)}) async-start(bf16[64,64,128]{2,1,0:T(8,128)(2,1)} %gather_fusion.3), calls=%async_computation.6 | async-start | bytes 2097152 | tf_op jit(solution)/shard_map/all_to_all | solution.py:181
  251.9 24.1 %copy-start.4 = (bf16[32,64,128]{2,1,0:T(8,128)(2,1)S(1)}, bf16[32,64,128]{2,1,0:T(8,128)(2,1)}, u32[]{:S(2)}) copy-start(bf16[32,64,128]{2,1,0:T(8,128)(2,1)} %gather_fusion.4) | copy-start | bytes 1572868
  319.6 6.5 %copy-start.1 = (f32[16,64,128]{2,1,0:T(8,128)S(1)}, f32[16,64,128]{2,1,0:T(8,128)}, u32[]{:S(2)}) copy-start(f32[16,64,128]{2,1,0:T(8,128)} %get-tuple-element.28) | copy-start | bytes 1572868
  319.6 6.5 %copy-start.2 = (f32[16,64,128]{2,1,0:T(8,128)S(1)}, f32[16,64,128]{2,1,0:T(8,128)}, u32[]{:S(2)}) copy-start(f32[16,64,128]{2,1,0:T(8,128)} %get-tuple-element.26) | copy-start | bytes 1572868
  321.8 33.7 %all-to-all-start.9 = ((bf16[16,128,128]{2,1,0:T(8,128)(2,1)}), bf16[16,128,128]{2,1,0:T(8,128)(2,1)}, u32[]{:S(2)}, u32[]{:S(2)}) async-start(bf16[16,128,128]{2,1,0:T(8,128)(2,1)} %copy.56), calls=%async_computation.9 | async-start | bytes 1048576 | tf_op jit(solution)/shard_map/all_to_all | solution.py:119
  326.8 5.5 %collective-permute-start.3 = (f32[16,128,1]{1,0,2:T(8,128)S(1)}, f32[16,128,1]{1,0,2:T(8,128)S(1)}, u32[]{:S(2)}, u32[]{:S(2)}) collective-permute-start(f32[16,128,1]{1,0,2:T(8,128)S(1)} %copy.58), channel_id=1, source_target_pairs={{1,0},{2,1},{3,2},{4,3},{5,4},{6,5},{7,6},{8,7},{9,8},{10,9},{11,1... | collective-permute-start | bytes 24584 | tf_op jit(solution)/shard_map/ppermute | solution.py:20
  330.2 5.0 %collective-permute-start.2 = (f32[16,128,1]{1,0,2:T(8,128)S(1)}, f32[16,128,1]{1,0,2:T(8,128)S(1)}, u32[]{:S(2)}, u32[]{:S(2)}) collective-permute-start(f32[16,128,1]{1,0,2:T(8,128)S(1)} %copy.57), channel_id=1, source_target_pairs={{0,1},{1,2},{2,3},{3,4},{4,5},{5,6},{6,7},{7,8},{8,9},{9,10},{10,1... | collective-permute-start | bytes 24584 | tf_op jit(solution)/shard_map/ppermute | solution.py:18
where the time goes:
time: 393 us; the launch traced here: 392 us
  blocking collectives  154 us (39%)
  waiting for transfers between devices  100 us (25%)
  starting transfers between devices  65.9 us (17%)
  local copies, waits for them, and re-layouts  26.6 us (7%)
  matrix products  26.3 us (7%)
  other arithmetic  18.5 us (5%)
    all_to_all x3, waiting for transfers between devices, exchange(): lax.all_to_all(payload, 'exp', split_axis=0, concat_axis=0, tiled=True)  47.8 us
    all_gather x1, blocking collectives, per_device(): gathered_head = lax.all_gather(scaled_head, 'exp', axis=0, tiled=True)  33.8 us
    all_gather x1, blocking collectives, per_device(): gathered = lax.all_gather(scaled, 'exp', axis=0, tiled=True)  33.7 us
    all_to_all x1, blocking collectives, exchange(): lax.all_to_all(outgoing_rows, 'sky', split_axis=0, concat_axis=0, tiled=T...  31.9 us
    all_gather x1, blocking collectives, per_device(): gathered_tail = lax.all_gather(scaled_tail, 'exp', axis=0, tiled=True)  31.1 us
    all_to_all x1, blocking collectives, fetch(): lax.all_to_all(part.astype(jnp.bfloat16)[safe_rows], 'sky', split_axis=0,...  23.4 us
    all_to_all x1, waiting for transfers between devices, fetch(): lax.all_to_all(part.astype(jnp.bfloat16)[safe_rows], 'sky', split_axis=0,...  23.1 us
    all_to_all x3, starting transfers between devices, exchange(): lax.all_to_all(payload, 'exp', split_axis=0, concat_axis=0, tiled=True)  22.1 us
  transfers between devices with their start and end apart: 12, of which 8 were waited for; matrix products, arithmetic and copies ran while one was open for 6% of the time, Pallas kernels for 0%

commit v1 on v0

--- a/solution.py
+++ b/solution.py
@@ -161,7 +161,25 @@
         scaled_head, outgoing_tail = lax.optimization_barrier(
             (scaled_head, outgoing[:, half_edge:])
         )
-        gathered_head = lax.all_gather(scaled_head, "exp", axis=0, tiled=True)
+
+        def take_the_numbers(local_x, a_name, at_axis):
+            size_here = lax.axis_size(a_name)
+            pieces_in = [local_x]
+            for j in [*range(size_here - 1)]:
+                small = lax.ppermute(
+                    pieces_in[-1],
+                    a_name,
+                    [(dev_i, (dev_i + 1) % size_here) for dev_i in range(size_here)],
+                )
+                pieces_in.append(small)
+            newest = jnp.roll(
+                jnp.concatenate(pieces_in[::-1], axis=at_axis),
+                shift=(lax.axis_index(a_name) + 1) * local_x.shape[at_axis],
+                axis=at_axis,
+            )
+            return newest
+
+        gathered_head = take_the_numbers(scaled_head, "exp", 0)
         arrived_tail = lax.all_to_all(outgoing_tail, "sky", split_axis=0, concat_axis=0, tiled=True)
         gathered_head, arrived_tail = lax.optimization_barrier((gathered_head, arrived_tail))
         scaled_tail = gather_scaled(exchange(arrived_tail, None, True), own_denominator)

time: 393 us -> 471 us (1.20)
  waiting for transfers between devices: 100 us -> 178 us
  blocking collectives: 154 us -> 121 us
  starting transfers between devices: 65.9 us -> 96.8 us
    ppermute x0 -> x15, waiting for transfers between devices: none -> 63.7 us  [take_the_numbers(): lax.ppermute(pieces_in[-1], a_name, [(dev_i, (dev_i + 1) % size_here) for...]
    all_gather x1 -> x0, blocking collectives: 33.8 us -> none  [per_device(): gathered_head = lax.all_gather(scaled_head, 'exp', axis=0, tiled=True)]
    ppermute x0 -> x15, starting transfers between devices: none -> 29.8 us  [take_the_numbers(): lax.ppermute(pieces_in[-1], a_name, [(dev_i, (dev_i + 1) % size_here) for...]
    all_to_all x1, waiting for transfers between devices: 0.01 us -> 15 us  [per_device(): lax.all_to_all(outgoing_tail, 'sky', split_axis=0, concat_axis=0, tiled=T...]
    ppermute x2, waiting for transfers between devices: 6.37 us -> 0.01 us  [padded_2(): lax.ppermute(head, axis, [((i + 1) % count, i) for i in range(ends)])]
  transfers between devices with their start and end apart: 12 -> 27, of which waited for: 8 -> 22; matrix products, arithmetic and copies ran while one was open for 6% -> 5% of each run, Pallas kernels for 0% -> 0%
where the time goes in v1:
time: 471 us; the launch traced here: 469 us
  waiting for transfers between devices  178 us (38%)
  blocking collectives  121 us (26%)
  starting transfers between devices  96.8 us (21%)
  local copies, waits for them, and re-layouts  27.8 us (6%)
  matrix products  26.4 us (6%)
  other arithmetic  18.7 us (4%)
    ppermute x15, waiting for transfers between devices, take_the_numbers(): lax.ppermute(pieces_in[-1], a_name, [(dev_i, (dev_i + 1) % size_here) for...  63.7 us
    all_to_all x3, waiting for transfers between devices, exchange(): lax.all_to_all(payload, 'exp', split_axis=0, concat_axis=0, tiled=True)  52.3 us
    all_gather x1, blocking collectives, per_device(): gathered = lax.all_gather(scaled, 'exp', axis=0, tiled=True)  33.6 us
    all_to_all x1, blocking collectives, exchange(): lax.all_to_all(outgoing_rows, 'sky', split_axis=0, concat_axis=0, tiled=T...  31.9 us
    all_gather x1, blocking collectives, per_device(): gathered_tail = lax.all_gather(scaled_tail, 'exp', axis=0, tiled=True)  31.6 us
    ppermute x15, starting transfers between devices, take_the_numbers(): lax.ppermute(pieces_in[-1], a_name, [(dev_i, (dev_i + 1) % size_here) for...  29.8 us
    all_to_all x3, starting transfers between devices, exchange(): lax.all_to_all(payload, 'exp', split_axis=0, concat_axis=0, tiled=True)  25.5 us
    all_to_all x1, blocking collectives, fetch(): lax.all_to_all(part.astype(jnp.bfloat16)[safe_rows], 'sky', split_axis=0,...  23.5 us
  transfers between devices with their start and end apart: 27, of which 22 were waited for; matrix products, arithmetic and copies ran while one was open for 5% of the time, Pallas kernels for 0%

profile of v1, /device:TPU:2, one launch (start us, length us, event | category | flops | bytes accessed | tf_op | source)
XLA Modules:
  0.0 469.4 jit_solution(5401360481071644027)
XLA Ops:
  3.8 9.4 %all-to-all-start = ((s32[32,2,1]{1,2,0:T(1,128)}), s32[32,2,1]{1,2,0:T(1,128)S(1)}, u32[]{:S(2)}, u32[]{:S(2)}) async-start(s32[32,2,1]{1,2,0:T(1,128)} %bitcast.2), calls=%async_computation | async-start | bytes 32768 | tf_op jit(solution)/shard_map/all_to_all | solution.py:94
  14.5 4.9 %all-to-all-done = s32[32,2,1]{1,2,0:T(1,128)S(1)} async-done(((s32[32,2,1]{1,2,0:T(1,128)}), s32[32,2,1]{1,2,0:T(1,128)S(1)}, u32[]{:S(2)}, u32[]{:S(2)}) %all-to-all-start) | async-done | bytes 288 | tf_op jit(solution)/shard_map/all_to_all | solution.py:94
  20.7 2.2 gather_fusion
  22.9 5.2 %all-to-all-start.1 = ((bf16[64,128,128]{2,1,0:T(8,128)(2,1)}), bf16[64,128,128]{2,1,0:T(8,128)(2,1)S(1)}, u32[]{:S(2)}, u32[]{:S(2)}) async-start(bf16[64,128,128]{2,1,0:T(8,128)(2,1)} %gather_fusion), calls=%async_computation.1 | async-start | bytes 4194304 | tf_op jit(solution)/shard_map/all_to_all | solution.py:123
  29.8 3.2 copy.72
  33.1 23.1 %all-to-all-done.1 = bf16[64,128,128]{2,1,0:T(8,128)(2,1)S(1)} async-done(((bf16[64,128,128]{2,1,0:T(8,128)(2,1)}), bf16[64,128,128]{2,1,0:T(8,128)(2,1)S(1)}, u32[]{:S(2)}, u32[]{:S(2)}) %all-to-all-start.1) | async-done | bytes 2097184 | tf_op jit(solution)/shard_map/all_to_all | solution.py:123
  56.9 6.4 %fusion.1 = bf16[32,2,128,128]{3,2,1,0:T(8,128)(2,1)} fusion(bf16[1,32,2,128,128]{4,3,2,1,0:T(8,128)(2,1)} %param.8, f32[32,2]{1,0:T(8,128)S(1)} %copy.43, bf16[32,2,2,128,128]{4,3,2,1,0:T(8,128)(2,1)} %bitcast.93, bf16[32,128,128]{2,1,0:T(8,128)(2,1)S(1)} %gather_fusion.1), kind=kOutput, calls=%fused_computation.12 | convolution fusion | flops 542113792 | bytes 9437440 | tf_op jit(solution)/shard_map/fetv,fewv->fetw/dot_general | solution.py:41
  63.2 4.3 bitcast_convert_fusion.1
  70.1 5.9 %all-to-all-start.2 = ((bf16[64,64,128]{2,1,0:T(8,128)(2,1)}), bf16[64,64,128]{2,1,0:T(8,128)(2,1)S(1)}, u32[]{:S(2)}, u32[]{:S(2)}) async-start(bf16[64,64,128]{2,1,0:T(8,128)(2,1)} %get-tuple-element.30), calls=%async_computation.2 | async-start | bytes 2097152 | tf_op jit(solution)/shard_map/all_to_all | solution.py:110
  76.4 15.9 %all-to-all-done.2 = bf16[64,64,128]{2,1,0:T(8,128)(2,1)S(1)} async-done(((bf16[64,64,128]{2,1,0:T(8,128)(2,1)}), bf16[64,64,128]{2,1,0:T(8,128)(2,1)S(1)}, u32[]{:S(2)}, u32[]{:S(2)}) %all-to-all-start.2) | async-done | bytes 1048608 | tf_op jit(solution)/shard_map/all_to_all | solution.py:110
  93.9 13.3 %all-to-all-start.3 = ((bf16[16,80,128]{2,1,0:T(8,128)(2,1)}), bf16[16,80,128]{2,1,0:T(8,128)(2,1)S(1)}, u32[]{:S(2)}, u32[]{:S(2)}) async-start(bf16[16,80,128]{2,1,0:T(8,128)(2,1)} %copy.47), calls=%async_computation.3 | async-start | bytes 655360 | tf_op jit(solution)/shard_map/all_to_all | solution.py:119
  107.2 21.4 %all-to-all-done.3 = bf16[16,80,128]{2,1,0:T(8,128)(2,1)S(1)} async-done(((bf16[16,80,128]{2,1,0:T(8,128)(2,1)}), bf16[16,80,128]{2,1,0:T(8,128)(2,1)S(1)}, u32[]{:S(2)}, u32[]{:S(2)}) %all-to-all-start.3) | async-done | bytes 327712 | tf_op jit(solution)/shard_map/all_to_all | solution.py:119
  130.1 2.9 collective-permute-start
  133.0 4.7 %collective-permute-done = bf16[1,64,128]{2,1,0:T(8,128)(2,1)S(1)} collective-permute-done((bf16[1,64,128]{2,1,0:T(8,128)(2,1)S(1)}, bf16[1,64,128]{2,1,0:T(8,128)(2,1)S(1)}, u32[]{:S(2)}, u32[]{:S(2)}) %collective-permute-start) | collective-permute-done | bytes 16416 | tf_op jit(solution)/shard_map/ppermute | solution.py:169
  139.6 4.9 %collective-permute-done.1 = bf16[1,64,128]{2,1,0:T(8,128)(2,1)S(1)} collective-permute-done((bf16[1,64,128]{2,1,0:T(8,128)(2,1)S(1)}, bf16[1,64,128]{2,1,0:T(8,128)(2,1)S(1)}, u32[]{:S(2)}, u32[]{:S(2)}) %collective-permute-start.1) | collective-permute-done | bytes 16416 | tf_op jit(solution)/shard_map/ppermute | solution.py:169
  144.6 1.9 collective-permute-start.2
  146.5 4.9 %collective-permute-done.2 = bf16[1,64,128]{2,1,0:T(8,128)(2,1)S(1)} collective-permute-done((bf16[1,64,128]{2,1,0:T(8,128)(2,1)S(1)}, bf16[1,64,128]{2,1,0:T(8,128)(2,1)S(1)}, u32[]{:S(2)}, u32[]{:S(2)}) %collective-permute-start.2) | collective-permute-done | bytes 16416 | tf_op jit(solution)/shard_map/ppermute | solution.py:169
  153.3 4.9 %collective-permute-done.3 = bf16[1,64,128]{2,1,0:T(8,128)(2,1)S(1)} collective-permute-done((bf16[1,64,128]{2,1,0:T(8,128)(2,1)S(1)}, bf16[1,64,128]{2,1,0:T(8,128)(2,1)S(1)}, u32[]{:S(2)}, u32[]{:S(2)}) %collective-permute-start.3) | collective-permute-done | bytes 16416 | tf_op jit(solution)/shard_map/ppermute | solution.py:169
  160.1 4.9 %collective-permute-done.4 = bf16[1,64,128]{2,1,0:T(8,128)(2,1)S(1)} collective-permute-done((bf16[1,64,128]{2,1,0:T(8,128)(2,1)S(1)}, bf16[1,64,128]{2,1,0:T(8,128)(2,1)S(1)}, u32[]{:S(2)}, u32[]{:S(2)}) %collective-permute-start.4) | collective-permute-done | bytes 16416 | tf_op jit(solution)/shard_map/ppermute | solution.py:169
  167.0 4.9 %collective-permute-done.5 = bf16[1,64,128]{2,1,0:T(8,128)(2,1)S(1)} collective-permute-done((bf16[1,64,128]{2,1,0:T(8,128)(2,1)S(1)}, bf16[1,64,128]{2,1,0:T(8,128)(2,1)S(1)}, u32[]{:S(2)}, u32[]{:S(2)}) %collective-permute-start.5) | collective-permute-done | bytes 16416 | tf_op jit(solution)/shard_map/ppermute | solution.py:169
  173.8 4.9 %collective-permute-done.6 = bf16[1,64,128]{2,1,0:T(8,128)(2,1)S(1)} collective-permute-done((bf16[1,64,128]{2,1,0:T(8,128)(2,1)S(1)}, bf16[1,64,128]{2,1,0:T(8,128)(2,1)S(1)}, u32[]{:S(2)}, u32[]{:S(2)}) %collective-permute-start.6) | collective-permute-done | bytes 16416 | tf_op jit(solution)/shard_map/ppermute | solution.py:169
  180.6 4.9 %collective-permute-done.7 = bf16[1,64,128]{2,1,0:T(8,128)(2,1)S(1)} collective-permute-done((bf16[1,64,128]{2,1,0:T(8,128)(2,1)S(1)}, bf16[1,64,128]{2,1,0:T(8,128)(2,1)S(1)}, u32[]{:S(2)}, u32[]{:S(2)}) %collective-permute-start.7) | collective-permute-done | bytes 16416 | tf_op jit(solution)/shard_map/ppermute | solution.py:169
  187.5 4.9 %collective-permute-done.8 = bf16[1,64,128]{2,1,0:T(8,128)(2,1)S(1)} collective-permute-done((bf16[1,64,128]{2,1,0:T(8,128)(2,1)S(1)}, bf16[1,64,128]{2,1,0:T(8,128)(2,1)S(1)}, u32[]{:S(2)}, u32[]{:S(2)}) %collective-permute-start.8) | collective-permute-done | bytes 16416 | tf_op jit(solution)/shard_map/ppermute | solution.py:169
  194.3 4.9 %collective-permute-done.9 = bf16[1,64,128]{2,1,0:T(8,128)(2,1)S(1)} collective-permute-done((bf16[1,64,128]{2,1,0:T(8,128)(2,1)S(1)}, bf16[1,64,128]{2,1,0:T(8,128)(2,1)S(1)}, u32[]{:S(2)}, u32[]{:S(2)}) %collective-permute-start.9) | collective-permute-done | bytes 16416 | tf_op jit(solution)/shard_map/ppermute | solution.py:169
  201.1 4.9 %collective-permute-done.10 = bf16[1,64,128]{2,1,0:T(8,128)(2,1)S(1)} collective-permute-done((bf16[1,64,128]{2,1,0:T(8,128)(2,1)S(1)}, bf16[1,64,128]{2,1,0:T(8,128)(2,1)S(1)}, u32[]{:S(2)}, u32[]{:S(2)}) %collective-permute-start.10) | collective-permute-done | bytes 16416 | tf_op jit(solution)/shard_map/ppermute | solution.py:169
  208.0 4.9 %collective-permute-done.11 = bf16[1,64,128]{2,1,0:T(8,128)(2,1)S(1)} collective-permute-done((bf16[1,64,128]{2,1,0:T(8,128)(2,1)S(1)}, bf16[1,64,128]{2,1,0:T(8,128)(2,1)S(1)}, u32[]{:S(2)}, u32[]{:S(2)}) %collective-permute-start.11) | collective-permute-done | bytes 16416 | tf_op jit(solution)/shard_map/ppermute | solution.py:169
  214.8 4.9 %collective-permute-done.12 = bf16[1,64,128]{2,1,0:T(8,128)(2,1)S(1)} collective-permute-done((bf16[1,64,128]{2,1,0:T(8,128)(2,1)S(1)}, bf16[1,64,128]{2,1,0:T(8,128)(2,1)S(1)}, u32[]{:S(2)}, u32[]{:S(2)}) %collective-permute-start.12) | collective-permute-done | bytes 16416 | tf_op jit(solution)/shard_map/ppermute | solution.py:169
  222.3 1.9 collective-permute-start.16
  224.6 2.4 collective-permute-start.15
  230.9 2.1 collective-permute-start.14
  233.0 2.4 pad_maximum_fusion
  236.8 6.6 %all-to-all-start.4 = ((bf16[64,64,128]{2,1,0:T(8,128)(2,1)}), bf16[64,64,128]{2,1,0:T(8,128)(2,1)}, u32[]{:S(2)}, u32[]{:S(2)}) async-start(bf16[64,64,128]{2,1,0:T(8,128)(2,1)} %get-tuple-element.14), calls=%async_computation.4 | async-start | bytes 2097152 | tf_op jit(solution)/shard_map/all_to_all | solution.py:183
  244.5 15.0 %all-to-all-done.4 = bf16[64,64,128]{2,1,0:T(8,128)(2,1)} async-done(((bf16[64,64,128]{2,1,0:T(8,128)(2,1)}), bf16[64,64,128]{2,1,0:T(8,128)(2,1)}, u32[]{:S(2)}, u32[]{:S(2)}) %all-to-all-start.4) | async-done | bytes 1048608 | tf_op jit(solution)/shard_map/all_to_all | solution.py:183
  262.2 7.8 %all-to-all-start.5 = ((bf16[16,64,128]{2,1,0:T(8,128)(2,1)}), bf16[16,64,128]{2,1,0:T(8,128)(2,1)S(1)}, u32[]{:S(2)}, u32[]{:S(2)}) async-start(bf16[16,64,128]{2,1,0:T(8,128)(2,1)} %copy.53), calls=%async_computation.5 | async-start | bytes 524288 | tf_op jit(solution)/shard_map/all_to_all | solution.py:119
  270.0 2.5 fusion.36
  276.0 12.5 %all-to-all-done.5 = bf16[16,64,128]{2,1,0:T(8,128)(2,1)S(1)} async-done(((bf16[16,64,128]{2,1,0:T(8,128)(2,1)}), bf16[16,64,128]{2,1,0:T(8,128)(2,1)S(1)}, u32[]{:S(2)}, u32[]{:S(2)}) %all-to-all-start.5) | async-done | bytes 262176 | tf_op jit(solution)/shard_map/all_to_all | solution.py:119
  289.3 5.0 %all-to-all-start.6 = ((bf16[64,64,128]{2,1,0:T(8,128)(2,1)}), bf16[64,64,128]{2,1,0:T(8,128)(2,1)S(1)}, u32[]{:S(2)}, u32[]{:S(2)}) async-start(bf16[64,64,128]{2,1,0:T(8,128)(2,1)} %gather_fusion.3), calls=%async_computation.6 | async-start | bytes 2097152 | tf_op jit(solution)/shard_map/all_to_all | solution.py:199
  294.3 31.6 %all_gather.6 = bf16[16,64,128]{2,1,0:T(8,128)(2,1)S(1)} all-gather(bf16[1,64,128]{2,1,0:T(8,128)(2,1)S(1)} %fusion.52), channel_id=1, replica_groups=mesh['exp'=16,'sky'=32] {'exp'}, dimensions={0}, use_global_device_ids=true | all-gather | bytes 278528 | tf_op jit(solution)/shard_map/all_gather | solution.py:198
  329.0 23.5 %all_to_all.51 = bf16[64,64,128]{2,1,0:T(8,128)(2,1)S(1)} all-to-all(bf16[64,64,128]{2,1,0:T(8,128)(2,1)S(1)} %gather_fusion.5), channel_id=1, replica_groups=mesh['exp'=16,'sky'=32] {'sky'}, dimensions={0} | all-to-all | bytes 2097152 | tf_op jit(solution)/shard_map/all_to_all | solution.py:123
  353.2 6.4 %fusion.3 = bf16[32,2,128,128]{3,2,1,0:T(8,128)(2,1)} fusion(bf16[1,32,2,128,128]{4,3,2,1,0:T(8,128)(2,1)} %param.8, f32[32,2]{1,0:T(8,128)S(1)} %copy.43, bf16[32,2,2,128,128]{4,3,2,1,0:T(8,128)(2,1)} %bitcast.95, bf16[32,64,128]{2,1,0:T(8,128)(2,1)S(1)} %gather_fusion.6, bf16[32,64,128]{2,1,0:T(8,128)(2,1)S(1)} %copy-done.4), kind=kOutput, calls=%fused_computation.14 | convolution fusion | flops 544210944 | bytes 9437440 | tf_op jit(solution)/shard_map/fetv,fewv->fetw/dot_general | solution.py:41
  359.5 4.3 bitcast_convert_fusion
  364.9 31.9 %all_to_all.52 = bf16[64,128,128]{2,1,0:T(8,128)(2,1)S(1)} all-to-all(bf16[64,128,128]{2,1,0:T(8,128)(2,1)S(1)} %gather_fusion.7), channel_id=1, replica_groups=mesh['exp'=16,'sky'=32] {'sky'}, dimensions={0} | all-to-all | bytes 4194304 | tf_op jit(solution)/shard_map/all_to_all | solution.py:110
  399.0 4.4 all-to-all-start.9
  404.1 2.9 collective-permute-start.18
  407.4 2.1 collective-permute-start.17
  409.9 2.4 collective-permute-done.17
  414.5 18.3 %all-to-all-done.9 = bf16[16,128,128]{2,1,0:T(8,128)(2,1)} async-done(((bf16[16,128,128]{2,1,0:T(8,128)(2,1)}), bf16[16,128,128]{2,1,0:T(8,128)(2,1)}, u32[]{:S(2)}, u32[]{:S(2)}) %all-to-all-start.9) | async-done | bytes 524320 | tf_op jit(solution)/shard_map/all_to_all | solution.py:119
  434.6 33.6 %all-gather = bf16[2048,128]{1,0:T(8,128)(2,1)S(1)} all-gather(bf16[128,128]{1,0:T(8,128)(2,1)S(1)} %divide_convert_fusion), channel_id=2, replica_groups=mesh['exp'=16,'sky'=32] {'exp'}, dimensions={0}, use_global_device_ids=true | all-gather | bytes 557056 | tf_op jit(solution)/shard_map/all_gather | solution.py:156
  (138 shorter events, 65.4 us)
Async XLA Ops:
  3.8 15.6 %all-to-all-start = ((s32[32,2,1]{1,2,0:T(1,128)}), s32[32,2,1]{1,2,0:T(1,128)S(1)}, u32[]{:S(2)}, u32[]{:S(2)}) async-start(s32[32,2,1]{1,2,0:T(1,128)} %bitcast.2), calls=%async_computation | async-start | bytes 32768 | tf_op jit(solution)/shard_map/all_to_all | solution.py:94
  22.9 5.3 %copy-start.8 = (bf16[1,32,2]{1,2,0:T(2,128)(2,1)S(1)}, bf16[1,32,2]{1,2,0:T(2,128)(2,1)}, u32[]{:S(2)}) copy-start(bf16[1,32,2]{1,2,0:T(2,128)(2,1)} %param.9) | copy-start | bytes 388
  22.9 5.4 %copy-start.7 = (s32[1,32,2,2]{1,3,2,0:T(2,128)S(1)}, s32[1,32,2,2]{1,3,2,0:T(2,128)}, u32[]{:S(2)}) copy-start(s32[1,32,2,2]{1,3,2,0:T(2,128)} %param.12) | copy-start | bytes 1540
  22.9 5.6 %copy-start.5 = (bf16[8,128,128]{2,1,0:T(8,128)(2,1)S(1)}, bf16[8,128,128]{2,1,0:T(8,128)(2,1)}, u32[]{:S(2)}) copy-start(bf16[8,128,128]{2,1,0:T(8,128)(2,1)} %param.13) | copy-start | bytes 786436
  22.9 33.2 %all-to-all-start.1 = ((bf16[64,128,128]{2,1,0:T(8,128)(2,1)}), bf16[64,128,128]{2,1,0:T(8,128)(2,1)S(1)}, u32[]{:S(2)}, u32[]{:S(2)}) async-start(bf16[64,128,128]{2,1,0:T(8,128)(2,1)} %gather_fusion), calls=%async_computation.1 | async-start | bytes 4194304 | tf_op jit(solution)/shard_map/all_to_all | solution.py:123
  29.8 3.2 copy-start.6
  70.1 22.2 %all-to-all-start.2 = ((bf16[64,64,128]{2,1,0:T(8,128)(2,1)}), bf16[64,64,128]{2,1,0:T(8,128)(2,1)S(1)}, u32[]{:S(2)}, u32[]{:S(2)}) async-start(bf16[64,64,128]{2,1,0:T(8,128)(2,1)} %get-tuple-element.30), calls=%async_computation.2 | async-start | bytes 2097152 | tf_op jit(solution)/shard_map/all_to_all | solution.py:110
  76.1 145.6 %copy-start = (f32[16,128,128]{2,1,0:T(8,128)S(1)}, f32[16,128,128]{2,1,0:T(8,128)}, u32[]{:S(2)}) copy-start(f32[16,128,128]{2,1,0:T(8,128)} %param.7) | copy-start | bytes 3145732
  93.9 34.7 %all-to-all-start.3 = ((bf16[16,80,128]{2,1,0:T(8,128)(2,1)}), bf16[16,80,128]{2,1,0:T(8,128)(2,1)S(1)}, u32[]{:S(2)}, u32[]{:S(2)}) async-start(bf16[16,80,128]{2,1,0:T(8,128)(2,1)} %copy.47), calls=%async_computation.3 | async-start | bytes 655360 | tf_op jit(solution)/shard_map/all_to_all | solution.py:119
  130.1 7.6 %collective-permute-start = (bf16[1,64,128]{2,1,0:T(8,128)(2,1)S(1)}, bf16[1,64,128]{2,1,0:T(8,128)(2,1)S(1)}, u32[]{:S(2)}, u32[]{:S(2)}) collective-permute-start(bf16[1,64,128]{2,1,0:T(8,128)(2,1)S(1)} %fusion.53), channel_id=1, source_target_pairs={{0,32},{32,64},{64,96},{96,128},{128,160},{160,192},{192,224},{224... | collective-permute-start | bytes 49160 | tf_op jit(solution)/shard_map/ppermute | solution.py:169
  137.7 6.8 %collective-permute-start.1 = (bf16[1,64,128]{2,1,0:T(8,128)(2,1)S(1)}, bf16[1,64,128]{2,1,0:T(8,128)(2,1)S(1)}, u32[]{:S(2)}, u32[]{:S(2)}) collective-permute-start(bf16[1,64,128]{2,1,0:T(8,128)(2,1)S(1)} %collective-permute-done), channel_id=1, source_target_pairs={{0,32},{32,64},{64,96},{96,128},{128,160},{160,192},{192,224},{224... | collective-permute-start | bytes 49160 | tf_op jit(solution)/shard_map/ppermute | solution.py:169
  144.6 6.8 %collective-permute-start.2 = (bf16[1,64,128]{2,1,0:T(8,128)(2,1)S(1)}, bf16[1,64,128]{2,1,0:T(8,128)(2,1)S(1)}, u32[]{:S(2)}, u32[]{:S(2)}) collective-permute-start(bf16[1,64,128]{2,1,0:T(8,128)(2,1)S(1)} %collective-permute-done.1), channel_id=1, source_target_pairs={{0,32},{32,64},{64,96},{96,128},{128,160},{160,192},{192,224},{224... | collective-permute-start | bytes 49160 | tf_op jit(solution)/shard_map/ppermute | solution.py:169
  151.4 6.8 %collective-permute-start.3 = (bf16[1,64,128]{2,1,0:T(8,128)(2,1)S(1)}, bf16[1,64,128]{2,1,0:T(8,128)(2,1)S(1)}, u32[]{:S(2)}, u32[]{:S(2)}) collective-permute-start(bf16[1,64,128]{2,1,0:T(8,128)(2,1)S(1)} %collective-permute-done.2), channel_id=1, source_target_pairs={{0,32},{32,64},{64,96},{96,128},{128,160},{160,192},{192,224},{224... | collective-permute-start | bytes 49160 | tf_op jit(solution)/shard_map/ppermute | solution.py:169
  158.2 6.8 %collective-permute-start.4 = (bf16[1,64,128]{2,1,0:T(8,128)(2,1)S(1)}, bf16[1,64,128]{2,1,0:T(8,128)(2,1)S(1)}, u32[]{:S(2)}, u32[]{:S(2)}) collective-permute-start(bf16[1,64,128]{2,1,0:T(8,128)(2,1)S(1)} %collective-permute-done.3), channel_id=1, source_target_pairs={{0,32},{32,64},{64,96},{96,128},{128,160},{160,192},{192,224},{224... | collective-permute-start | bytes 49160 | tf_op jit(solution)/shard_map/ppermute | solution.py:169
  165.1 6.8 %collective-permute-start.5 = (bf16[1,64,128]{2,1,0:T(8,128)(2,1)S(1)}, bf16[1,64,128]{2,1,0:T(8,128)(2,1)S(1)}, u32[]{:S(2)}, u32[]{:S(2)}) collective-permute-start(bf16[1,64,128]{2,1,0:T(8,128)(2,1)S(1)} %collective-permute-done.4), channel_id=1, source_target_pairs={{0,32},{32,64},{64,96},{96,128},{128,160},{160,192},{192,224},{224... | collective-permute-start | bytes 49160 | tf_op jit(solution)/shard_map/ppermute | solution.py:169
  171.9 6.8 %collective-permute-start.6 = (bf16[1,64,128]{2,1,0:T(8,128)(2,1)S(1)}, bf16[1,64,128]{2,1,0:T(8,128)(2,1)S(1)}, u32[]{:S(2)}, u32[]{:S(2)}) collective-permute-start(bf16[1,64,128]{2,1,0:T(8,128)(2,1)S(1)} %collective-permute-done.5), channel_id=1, source_target_pairs={{0,32},{32,64},{64,96},{96,128},{128,160},{160,192},{192,224},{224... | collective-permute-start | bytes 49160 | tf_op jit(solution)/shard_map/ppermute | solution.py:169
  178.7 6.8 %collective-permute-start.7 = (bf16[1,64,128]{2,1,0:T(8,128)(2,1)S(1)}, bf16[1,64,128]{2,1,0:T(8,128)(2,1)S(1)}, u32[]{:S(2)}, u32[]{:S(2)}) collective-permute-start(bf16[1,64,128]{2,1,0:T(8,128)(2,1)S(1)} %collective-permute-done.6), channel_id=1, source_target_pairs={{0,32},{32,64},{64,96},{96,128},{128,160},{160,192},{192,224},{224... | collective-permute-start | bytes 49160 | tf_op jit(solution)/shard_map/ppermute | solution.py:169
  185.6 6.8 %collective-permute-start.8 = (bf16[1,64,128]{2,1,0:T(8,128)(2,1)S(1)}, bf16[1,64,128]{2,1,0:T(8,128)(2,1)S(1)}, u32[]{:S(2)}, u32[]{:S(2)}) collective-permute-start(bf16[1,64,128]{2,1,0:T(8,128)(2,1)S(1)} %collective-permute-done.7), channel_id=1, source_target_pairs={{0,32},{32,64},{64,96},{96,128},{128,160},{160,192},{192,224},{224... | collective-permute-start | bytes 49160 | tf_op jit(solution)/shard_map/ppermute | solution.py:169
  192.4 6.8 %collective-permute-start.9 = (bf16[1,64,128]{2,1,0:T(8,128)(2,1)S(1)}, bf16[1,64,128]{2,1,0:T(8,128)(2,1)S(1)}, u32[]{:S(2)}, u32[]{:S(2)}) collective-permute-start(bf16[1,64,128]{2,1,0:T(8,128)(2,1)S(1)} %collective-permute-done.8), channel_id=1, source_target_pairs={{0,32},{32,64},{64,96},{96,128},{128,160},{160,192},{192,224},{224... | collective-permute-start | bytes 49160 | tf_op jit(solution)/shard_map/ppermute | solution.py:169
  199.2 6.8 %collective-permute-start.10 = (bf16[1,64,128]{2,1,0:T(8,128)(2,1)S(1)}, bf16[1,64,128]{2,1,0:T(8,128)(2,1)S(1)}, u32[]{:S(2)}, u32[]{:S(2)}) collective-permute-start(bf16[1,64,128]{2,1,0:T(8,128)(2,1)S(1)} %collective-permute-done.9), channel_id=1, source_target_pairs={{0,32},{32,64},{64,96},{96,128},{128,160},{160,192},{192,224},{224... | collective-permute-start | bytes 49160 | tf_op jit(solution)/shard_map/ppermute | solution.py:169
  206.1 6.8 %collective-permute-start.11 = (bf16[1,64,128]{2,1,0:T(8,128)(2,1)S(1)}, bf16[1,64,128]{2,1,0:T(8,128)(2,1)S(1)}, u32[]{:S(2)}, u32[]{:S(2)}) collective-permute-start(bf16[1,64,128]{2,1,0:T(8,128)(2,1)S(1)} %collective-permute-done.10), channel_id=1, source_target_pairs={{0,32},{32,64},{64,96},{96,128},{128,160},{160,192},{192,224},{224... | collective-permute-start | bytes 49160 | tf_op jit(solution)/shard_map/ppermute | solution.py:169
  212.9 6.8 %collective-permute-start.12 = (bf16[1,64,128]{2,1,0:T(8,128)(2,1)S(1)}, bf16[1,64,128]{2,1,0:T(8,128)(2,1)S(1)}, u32[]{:S(2)}, u32[]{:S(2)}) collective-permute-start(bf16[1,64,128]{2,1,0:T(8,128)(2,1)S(1)} %collective-permute-done.11), channel_id=1, source_target_pairs={{0,32},{32,64},{64,96},{96,128},{128,160},{160,192},{192,224},{224... | collective-permute-start | bytes 49160 | tf_op jit(solution)/shard_map/ppermute | solution.py:169
  219.7 11.2 %collective-permute-start.13 = (bf16[1,64,128]{2,1,0:T(8,128)(2,1)S(1)}, bf16[1,64,128]{2,1,0:T(8,128)(2,1)S(1)}, u32[]{:S(2)}, u32[]{:S(2)}) collective-permute-start(bf16[1,64,128]{2,1,0:T(8,128)(2,1)S(1)} %collective-permute-done.12), channel_id=1, source_target_pairs={{0,32},{32,64},{64,96},{96,128},{128,160},{160,192},{192,224},{224... | collective-permute-start | bytes 49160 | tf_op jit(solution)/shard_map/ppermute | solution.py:169
  222.3 4.7 %collective-permute-start.16 = (f32[16,128,1]{1,0,2:T(8,128)S(1)}, f32[16,128,1]{1,0,2:T(8,128)S(1)}, u32[]{:S(2)}, u32[]{:S(2)}) collective-permute-start(f32[16,128,1]{1,0,2:T(8,128)S(1)} %copy.70), channel_id=1, source_target_pairs={{1,0},{2,1},{3,2},{4,3},{5,4},{6,5},{7,6},{8,7},{9,8},{10,9},{11,1... | collective-permute-start | bytes 24584 | tf_op jit(solution)/shard_map/ppermute | solution.py:20
  224.6 5.0 %collective-permute-start.15 = (f32[16,128,1]{1,0,2:T(8,128)S(1)}, f32[16,128,1]{1,0,2:T(8,128)S(1)}, u32[]{:S(2)}, u32[]{:S(2)}) collective-permute-start(f32[16,128,1]{1,0,2:T(8,128)S(1)} %copy.69), channel_id=1, source_target_pairs={{0,1},{1,2},{2,3},{3,4},{4,5},{5,6},{6,7},{7,8},{8,9},{9,10},{10,1... | collective-permute-start | bytes 24584 | tf_op jit(solution)/shard_map/ppermute | solution.py:18
  230.9 12.4 %collective-permute-start.14 = (bf16[1,64,128]{2,1,0:T(8,128)(2,1)S(1)}, bf16[1,64,128]{2,1,0:T(8,128)(2,1)S(1)}, u32[]{:S(2)}, u32[]{:S(2)}) collective-permute-start(bf16[1,64,128]{2,1,0:T(8,128)(2,1)S(1)} %collective-permute-done.13), channel_id=1, source_target_pairs={{0,32},{32,64},{64,96},{96,128},{128,160},{160,192},{192,224},{224... | collective-permute-start | bytes 49160 | tf_op jit(solution)/shard_map/ppermute | solution.py:169
  236.8 22.8 %all-to-all-start.4 = ((bf16[64,64,128]{2,1,0:T(8,128)(2,1)}), bf16[64,64,128]{2,1,0:T(8,128)(2,1)}, u32[]{:S(2)}, u32[]{:S(2)}) async-start(bf16[64,64,128]{2,1,0:T(8,128)(2,1)} %get-tuple-element.14), calls=%async_computation.4 | async-start | bytes 2097152 | tf_op jit(solution)/shard_map/all_to_all | solution.py:183
  262.2 26.3 %all-to-all-start.5 = ((bf16[16,64,128]{2,1,0:T(8,128)(2,1)}), bf16[16,64,128]{2,1,0:T(8,128)(2,1)S(1)}, u32[]{:S(2)}, u32[]{:S(2)}) async-start(bf16[16,64,128]{2,1,0:T(8,128)(2,1)} %copy.53), calls=%async_computation.5 | async-start | bytes 524288 | tf_op jit(solution)/shard_map/all_to_all | solution.py:119
  272.5 1.0 copy-start.3
  289.3 36.6 %all-to-all-start.6 = ((bf16[64,64,128]{2,1,0:T(8,128)(2,1)}), bf16[64,64,128]{2,1,0:T(8,128)(2,1)S(1)}, u32[]{:S(2)}, u32[]{:S(2)}) async-start(bf16[64,64,128]{2,1,0:T(8,128)(2,1)} %gather_fusion.3), calls=%async_computation.6 | async-start | bytes 2097152 | tf_op jit(solution)/shard_map/all_to_all | solution.py:199
  329.0 24.2 %copy-start.4 = (bf16[32,64,128]{2,1,0:T(8,128)(2,1)S(1)}, bf16[32,64,128]{2,1,0:T(8,128)(2,1)}, u32[]{:S(2)}) copy-start(bf16[32,64,128]{2,1,0:T(8,128)(2,1)} %gather_fusion.4) | copy-start | bytes 1572868
  396.8 6.6 %copy-start.1 = (f32[16,64,128]{2,1,0:T(8,128)S(1)}, f32[16,64,128]{2,1,0:T(8,128)}, u32[]{:S(2)}) copy-start(f32[16,64,128]{2,1,0:T(8,128)} %get-tuple-element.28) | copy-start | bytes 1572868
  396.8 6.6 %copy-start.2 = (f32[16,64,128]{2,1,0:T(8,128)S(1)}, f32[16,64,128]{2,1,0:T(8,128)}, u32[]{:S(2)}) copy-start(f32[16,64,128]{2,1,0:T(8,128)} %get-tuple-element.26) | copy-start | bytes 1572868
  399.0 33.8 %all-to-all-start.9 = ((bf16[16,128,128]{2,1,0:T(8,128)(2,1)}), bf16[16,128,128]{2,1,0:T(8,128)(2,1)}, u32[]{:S(2)}, u32[]{:S(2)}) async-start(bf16[16,128,128]{2,1,0:T(8,128)(2,1)} %copy.56), calls=%async_computation.9 | async-start | bytes 1048576 | tf_op jit(solution)/shard_map/all_to_all | solution.py:119
  404.1 5.4 %collective-permute-start.18 = (f32[16,128,1]{1,0,2:T(8,128)S(1)}, f32[16,128,1]{1,0,2:T(8,128)S(1)}, u32[]{:S(2)}, u32[]{:S(2)}) collective-permute-start(f32[16,128,1]{1,0,2:T(8,128)S(1)} %copy.58), channel_id=1, source_target_pairs={{1,0},{2,1},{3,2},{4,3},{5,4},{6,5},{7,6},{8,7},{9,8},{10,9},{11,1... | collective-permute-start | bytes 24584 | tf_op jit(solution)/shard_map/ppermute | solution.py:20
  407.4 5.0 %collective-permute-start.17 = (f32[16,128,1]{1,0,2:T(8,128)S(1)}, f32[16,128,1]{1,0,2:T(8,128)S(1)}, u32[]{:S(2)}, u32[]{:S(2)}) collective-permute-start(f32[16,128,1]{1,0,2:T(8,128)S(1)} %copy.57), channel_id=1, source_target_pairs={{0,1},{1,2},{2,3},{3,4},{4,5},{5,6},{6,7},{7,8},{8,9},{9,10},{10,1... | collective-permute-start | bytes 24584 | tf_op jit(solution)/shard_map/ppermute | solution.py:18
